TPU v7x, 256 devices: a whole 4x4x8 slice. The times are simulated.
256 devices in a mesh: row: 16 (over x, y_hi, core), col: 16 (over y_lo, z).
Axes of the slice: x: 4, y: 4 (y_hi: 2, y_lo: 2; y = y_hi * 2 + y_lo), z: 8, core: 2. Of those that a mesh axis runs over, the one named last changes fastest.
Arguments:
- left_rows: float32 [1024, 61440], P('col', 'row'), may hold values from -1.2 to 1.2
- right_cols: float32 [61440, 4096], P('col', 'row'), may hold values from -1.2 to 1.2
- left_pattern: int32 [16, 240], replicated, may hold values from 0 to 1, as said below
- right_pattern: int32 [240, 16], replicated, may hold values from 0 to 1, as said below
Outputs:
- square_terms: float32 [1024, 4096], P('col', 'row')
Inputs may be any that keep to these rules, and one draw needn't show every extreme that they name: Every device's tile of left_pattern (row b, inner blocks from a * 15) has between 1 and 3 occupied blocks, and some tile has exactly 3 in every draw. Every device's tile of right_pattern (inner blocks from b * 15, column a) has between 1 and 3 occupied blocks, and some tile has exactly 3 in every draw.
All inputs are finite; a program needn't handle non-finite values.
Results may differ from a plain program's by a relative error of at most 0.0001.
Values sent between devices are 32-bit elements; how exact they have to be, the bound alone decides.
No kernel may reach another device: no remote copies, remote signals or barrier semaphores. Data moves between devices by JAX's collectives and lax.ppermute only.
A program may use at most 128 MiB of HBM per device.

v0:
```python
import jax
import jax.numpy as jnp
from jax import lax
from jax.sharding import PartitionSpec as P

STEPS = 4
CAP = 3


def from_behind(value, axis, steps):
    count = lax.axis_size(axis)
    pairs = [(source, (source - steps) % count) for source in range(count)]
    return lax.ppermute(value, axis, pairs)


def occupied(flags, cap):
    flags = flags != 0
    rank = jnp.cumsum(flags.astype(jnp.int32)) - 1
    where = jnp.arange(flags.shape[0], dtype=jnp.int32)
    hit = flags[None, :] & (rank[None, :] == jnp.arange(cap, dtype=jnp.int32)[:, None])
    index = jnp.sum(jnp.where(hit, where[None, :], 0), axis=1)
    return (index, jnp.any(hit, axis=1))


def left_flags(left_pattern, block_row, block_col, per_k):
    return lax.dynamic_slice(left_pattern, (block_row, block_col * per_k), (1, per_k)).reshape(-1)


def right_flags(right_pattern, block_row, block_col, trows):
    return lax.dynamic_slice(right_pattern, (block_row * trows, block_col), (trows, 1)).reshape(-1)


def pick_cols(x, index, blk):
    return jnp.concatenate(
        [lax.dynamic_slice_in_dim(x, index[s] * blk, blk, axis=1) for s in range(index.shape[0])],
        axis=1,
    )


def pick_rows(x, index, blk):
    return jnp.concatenate(
        [lax.dynamic_slice_in_dim(x, index[s] * blk, blk, axis=0) for s in range(index.shape[0])],
        axis=0,
    )


def body(left_rows, right_cols, left_pattern, right_pattern):
    nrow = lax.axis_size("row")
    ncol = lax.axis_size("col")
    ratio = nrow // ncol
    lrows, left_width = left_rows.shape
    right_height, blk = right_cols.shape
    per_k = left_width // blk
    trows = right_height // blk
    rowdev = lax.axis_index("row")
    coldev = lax.axis_index("col")
    own_left, _ = occupied(left_flags(left_pattern, coldev, rowdev, per_k), CAP)
    own_right, _ = occupied(right_flags(right_pattern, coldev, rowdev, trows), CAP)
    left_small = pick_cols(left_rows, own_left, blk)
    right_small = pick_rows(right_cols, own_right, blk)
    roots = [(coldev * ratio + step) % nrow for step in range(STEPS)]
    slots = jnp.stack(
        [jnp.where(rowdev == root, left_small, jnp.zeros_like(left_small)) for root in roots]
    )
    lefts = lax.psum(slots, "row")
    total = jnp.zeros((lrows, blk), jnp.float32)
    highest = lax.Precision.HIGHEST
    for step in range(STEPS):
        shift = step // ratio
        right = right_small if shift == 0 else from_behind(right_small, "col", shift)
        panel = roots[step]
        lidx, lok = occupied(left_flags(left_pattern, coldev, panel, per_k), CAP)
        ridx, rok = occupied(
            right_flags(right_pattern, (coldev + shift) % ncol, rowdev, trows), CAP
        )
        match = ((lidx[:, None] == ridx[None, :]) & lok[:, None] & rok[None, :]).astype(jnp.float32)
        left = lefts[step]
        blocks = [left[:, i * blk : (i + 1) * blk] for i in range(CAP)]
        aligned = []
        for j in range(CAP):
            part = match[0, j] * blocks[0]
            for i in range(1, CAP):
                part = part + match[i, j] * blocks[i]
            aligned.append(part)
        aligned = jnp.concatenate(aligned, axis=1)
        total = total + jnp.dot(
            aligned, right, precision=highest, preferred_element_type=jnp.float32
        )
    return total


def solution(mesh):
    return jax.shard_map(
        body,
        mesh=mesh,
        in_specs=(P("col", "row"), P("col", "row"), P(), P()),
        out_specs=P("col", "row"),
        check_vma=False,
    )
```

profile of v0, /device:TPU:1, one launch (start us, length us, event | category | flops | bytes accessed | tf_op | source)
XLA Modules:
  0.0 217.3 jit_solution(2198795887849036355)
XLA Ops:
  6.5 1.0 compare_bitcast_fusion.3
  7.5 0.2 reduce-window.82
  7.7 1.0 compare_bitcast_fusion.2
  8.7 0.2 reduce-window.83
  8.8 0.1 select_reduce_fusion.6
  9.0 0.7 fusion.55
  11.7 1.2 constant_dynamic-slice_fusion.2
  12.8 0.1 pad_maximum_fusion.1
  12.9 7.5 %collective-permute-start = (f32[768,256]{1,0:T(8,128)S(1)}, f32[768,256]{1,0:T(8,128)S(1)}, u32[]{:S(2)}, u32[]{:S(2)}) collective-permute-start(f32[768,256]{1,0:T(8,128)S(1)} %pad_maximum_fusion.1), channel_id=1, source_target_pairs={{0,15},{1,0},{2,1},{3,2},{4,3},{5,4},{6,5},{7,6},{8,7},{9,8},{10,9... | collective-permute-start | bytes 2359304 | tf_op jit(solution)/shard_map/ppermute | solution.py:13
  20.4 1.6 collective-permute-start.2
  22.0 0.6 fusion.54
  24.6 0.9 dynamic-slice_bitcast_fusion.2
  25.5 0.1 broadcast_select_fusion.3
  25.6 0.9 pad_maximum_fusion
  26.6 0.2 reduce-window.84
  26.8 0.2 reduce-window.80
  27.0 0.2 reduce-window.85
  27.2 0.2 reduce-window.81
  27.4 0.1 fusion.38
  27.5 0.2 select_reduce_fusion.4
  27.7 0.2 fusion.37
  27.8 0.2 select_reduce_fusion.8
  28.0 0.2 reduce-window.88
  28.2 0.2 reduce-window.86
  28.4 0.2 reduce-window.87
  28.6 0.2 reduce-window.89
  28.8 0.2 fusion.34
  28.9 0.2 select_reduce_fusion.2
  29.1 0.2 fusion.33
  29.2 0.1 and_convert_fusion.1
  29.3 0.7 fusion.50
  30.0 0.1 and_convert_fusion.2
  30.1 0.1 select_reduce_fusion
  30.2 0.7 fusion.51
  30.9 0.1 and_convert_fusion.3
  31.0 0.7 fusion.52
  31.6 0.1 and_convert_fusion
  31.7 0.7 fusion.53
  32.4 150.2 %all-reduce.2.cloned.1.call-done = f32[4,64,768]{2,1,0:T(8,128)} async-done(((f32[4,64,768]{2,1,0:T(8,128)}), f32[4,64,768]{2,1,0:T(8,128)}) %all-reduce.2.cloned.1.call-update) | async-done | bytes 786448 | tf_op jit(solution)/shard_map/psum | solution.py:65
  182.6 1.3 slice_bitcast_fusion.1
  183.9 5.5 %multiply_add_fusion.5 = (f32[64,256]{1,0:T(8,128)S(1)}, f32[64,256]{1,0:T(8,128)S(1)}, f32[64,256]{1,0:T(8,128)S(1)}) fusion(f32[64,768]{1,0:T(8,128)S(1)} %get-tuple-element.11, f32[]{:T(128)} %bitcast.52, f32[]{:T(128)} %bitcast.51, f32[]{:T(128)} %bitcast.49, f32[]{:T(128)} %bitcast.55, f32[]{:T(128)} %bitcast.54, f32[]{:T(128)} %bitcast.53, ...), kind=kLoop, calls=%fused_computation.41 | loop fusion | flops 245760 | bytes 393252 | tf_op jit(solution)/shard_map/add | solution.py:83
  189.4 5.8 %multiply_add_fusion.8 = (f32[64,256]{1,0:T(8,128)S(1)}, f32[64,256]{1,0:T(8,128)S(1)}, f32[64,256]{1,0:T(8,128)S(1)}) fusion(f32[64,768]{1,0:T(8,128)S(1)} %get-tuple-element.13, f32[]{:T(128)} %bitcast.37, f32[]{:T(128)} %bitcast.36, f32[]{:T(128)} %bitcast.34, f32[]{:T(128)} %bitcast.40, f32[]{:T(128)} %bitcast.39, f32[]{:T(128)} %bitcast.38, ...), kind=kLoop, calls=%fused_computation.44 | loop fusion | flops 245760 | bytes 393252 | tf_op jit(solution)/shard_map/add | solution.py:83
  195.2 5.7 %multiply_add_fusion.11 = (f32[64,256]{1,0:T(8,128)S(1)}, f32[64,256]{1,0:T(8,128)S(1)}, f32[64,256]{1,0:T(8,128)S(1)}) fusion(f32[64,768]{1,0:T(8,128)S(1)} %get-tuple-element.14, f32[]{:T(128)} %bitcast.17, f32[]{:T(128)} %bitcast.16, f32[]{:T(128)} %bitcast.5, f32[]{:T(128)} %bitcast.20, f32[]{:T(128)} %bitcast.19, f32[]{:T(128)} %bitcast.18, ...), kind=kLoop, calls=%fused_computation.47 | loop fusion | flops 245760 | bytes 393252 | tf_op jit(solution)/shard_map/add | solution.py:83
  201.0 0.5 fusion.1
  201.5 5.6 %multiply_add_fusion.2 = (f32[64,256]{1,0:T(8,128)S(1)}, f32[64,256]{1,0:T(8,128)S(1)}, f32[64,256]{1,0:T(8,128)S(1)}) fusion(f32[64,768]{1,0:T(8,128)S(1)} %get-tuple-element.12, f32[]{:T(128)} %bitcast.67, f32[]{:T(128)} %bitcast.66, f32[]{:T(128)} %bitcast.64, f32[]{:T(128)} %bitcast.70, f32[]{:T(128)} %bitcast.69, f32[]{:T(128)} %bitcast.68, ...), kind=kLoop, calls=%fused_computation.38 | loop fusion | flops 245760 | bytes 393252 | tf_op jit(solution)/shard_map/add | solution.py:83
  207.1 1.6 fusion.17
  208.7 0.5 convolution_add_fusion.1
  209.3 1.1 fusion
  (16 shorter events, 0.1 us)
Async XLA Ops:
  6.5 176.1 %all-reduce.2.cloned.1.call-start = ((), (), s32[]{:S(2)}) async-start(), calls=%async_computation | async-start | bytes 1572864 | tf_op jit(solution)/shard_map/psum | solution.py:65
  12.9 195.8 %collective-permute-start = (f32[768,256]{1,0:T(8,128)S(1)}, f32[768,256]{1,0:T(8,128)S(1)}, u32[]{:S(2)}, u32[]{:S(2)}) collective-permute-start(f32[768,256]{1,0:T(8,128)S(1)} %pad_maximum_fusion.1), channel_id=1, source_target_pairs={{0,15},{1,0},{2,1},{3,2},{4,3},{5,4},{6,5},{7,6},{8,7},{9,8},{10,9... | collective-permute-start | bytes 2359304 | tf_op jit(solution)/shard_map/ppermute | solution.py:13
  20.4 186.7 %collective-permute-start.2 = (f32[768,256]{1,0:T(8,128)S(1)}, f32[768,256]{1,0:T(8,128)}, u32[]{:S(2)}, u32[]{:S(2)}) collective-permute-start(f32[768,256]{1,0:T(8,128)S(1)} %pad_maximum_fusion.1), channel_id=1, source_target_pairs={{0,13},{1,14},{2,15},{3,0},{4,1},{5,2},{6,3},{7,4},{8,5},{9,6},{10... | collective-permute-start | bytes 2359304 | tf_op jit(solution)/shard_map/ppermute | solution.py:13
  22.0 187.3 %collective-permute-start.1 = (f32[768,256]{1,0:T(8,128)S(1)}, f32[768,256]{1,0:T(8,128)S(1)}, u32[]{:S(2)}, u32[]{:S(2)}) collective-permute-start(f32[768,256]{1,0:T(8,128)S(1)} %pad_maximum_fusion.1), channel_id=1, source_target_pairs={{0,14},{1,15},{2,0},{3,1},{4,2},{5,3},{6,4},{7,5},{8,6},{9,7},{10,... | collective-permute-start | bytes 2359304 | tf_op jit(solution)/shard_map/ppermute | solution.py:13
Sparse Core Ops, SparseCore 0:
  26.7 155.8 all-reduce.1
where the time goes:
time: 218 us; the launch traced here: 217 us
  waiting for transfers between devices  150 us (69%)
  other arithmetic  29.2 us (13%)
  between operations  17.4 us (8%)
  starting transfers between devices  9.11 us (4%)
  local copies, waits for them, and re-layouts  7.41 us (3%)
  matrix products  3.81 us (2%)
    psum x1, waiting for transfers between devices, body(): lefts = lax.psum(slots, 'row')  150 us
    add x4, other arithmetic, body(): part = part + match[i, j] * blocks[i]  22.6 us
    ppermute x3, starting transfers between devices, from_behind(): return lax.ppermute(value, axis, pairs)  9.11 us
  transfers between devices with their start and end apart: 4, of which 1 were waited for; matrix products, arithmetic and copies ran while one was open for 16% of the time, Pallas kernels for 0%

commit v1 on v0

--- a/solution.py
+++ b/solution.py
@@ -62,7 +62,11 @@
     slots = jnp.stack(
         [jnp.where(rowdev == root, left_small, jnp.zeros_like(left_small)) for root in roots]
     )
-    lefts = lax.psum(slots, "row")
+
+    def modes_pair(arr_in):
+        return jnp.sum(lax.all_gather(arr_in, axis_name="row"), axis=0)
+
+    lefts = modes_pair(slots)
     total = jnp.zeros((lrows, blk), jnp.float32)
     highest = lax.Precision.HIGHEST
     for step in range(STEPS):

time: 218 us -> 187 us (0.86)
  the two profiles are of different devices: /device:TPU:1 before, /device:TPU:225 now
where the time goes in v1:
time: 187 us; the launch traced here: 186 us
  waiting for transfers between devices  121 us (65%)
  other arithmetic  34.8 us (19%)
  between operations  17.4 us (9%)
  local copies, waits for them, and re-layouts  6.26 us (3%)
  matrix products  4.94 us (3%)
  starting transfers between devices  1.96 us (1%)
    all_gather x1, waiting for transfers between devices, modes_pair(): return jnp.sum(lax.all_gather(arr_in, axis_name='row'), axis=0)  121 us
    add x4, other arithmetic, body(): part = part + match[i, j] * blocks[i]  22.8 us
    reduce_sum x1, other arithmetic, modes_pair(): return jnp.sum(lax.all_gather(arr_in, axis_name='row'), axis=0)  5.43 us
    dot_general x4, matrix products, body(): jnp.dot(aligned, right, precision=highest, preferred_element_type=jnp.flo...  4.94 us
  transfers between devices with their start and end apart: 4, of which 1 were waited for; matrix products, arithmetic and copies ran while one was open for 21% of the time, Pallas kernels for 0%

profile of v1, /device:TPU:225, one launch (start us, length us, event | category | flops | bytes accessed | tf_op | source)
XLA Modules:
  0.0 186.2 jit_solution(14499521365751892398)
XLA Ops:
  6.5 0.9 compare_bitcast_fusion.3
  7.5 0.2 reduce-window.82
  7.7 0.9 compare_bitcast_fusion.2
  8.6 0.2 reduce-window.83
  8.8 0.1 select_reduce_fusion.6
  9.0 0.7 fusion.54
  11.7 0.9 dynamic-slice_bitcast_fusion.2
  12.6 0.1 broadcast_select_fusion.3
  12.7 0.9 pad_maximum_fusion
  13.6 0.7 fusion.55
  16.2 1.2 constant_dynamic-slice_fusion.2
  17.4 0.8 collective-permute-start
  18.3 0.9 collective-permute-start.2
  19.2 0.2 collective-permute-start.1
  19.4 0.2 reduce-window.88
  19.6 0.2 reduce-window.86
  19.8 0.2 reduce-window.87
  20.0 0.2 reduce-window.89
  20.1 0.2 reduce-window.84
  20.3 0.2 reduce-window.80
  20.5 0.2 reduce-window.85
  20.7 0.2 reduce-window.81
  20.9 0.1 fusion.34
  21.1 0.1 fusion.33
  21.2 0.1 fusion.38
  21.4 0.1 fusion.37
  21.6 0.2 select_reduce_fusion.2
  21.7 0.2 select_reduce_fusion.4
  21.9 0.2 select_reduce_fusion.8
  22.0 0.2 select_reduce_fusion
  22.2 0.1 and_convert_fusion.1
  22.3 0.7 fusion.50
  22.9 0.1 and_convert_fusion.2
  23.0 0.7 fusion.51
  23.7 0.1 and_convert_fusion.3
  23.8 0.7 fusion.52
  24.5 0.1 and_convert_fusion
  24.5 0.7 fusion.53
  25.2 120.8 %all-gather.3.cloned.1.call-done = f32[64,64,768]{2,1,0:T(8,128)} async-done(((f32[4,64,768]{2,1,0:T(8,128)}), f32[64,64,768]{2,1,0:T(8,128)}) %all-gather.3.cloned.1.call-update) | async-done | bytes 12582928 | tf_op jit(solution)/shard_map/all_gather | solution.py:67
  146.0 5.4 %reduce_sum.102 = f32[4,64,768]{2,1,0:T(8,128)S(1)} reduce(f32[16,4,64,768]{3,2,1,0:T(8,128)} %bitcast.110, f32[]{:T(128)} %constant.86.clone.1), dimensions={0}, to_apply=%region_8.9 | reduce | flops 2949120 | bytes 13369348 | tf_op jit(solution)/shard_map/reduce_sum | solution.py:67
  151.5 5.7 %multiply_add_fusion.5 = (f32[64,256]{1,0:T(8,128)S(1)}, f32[64,256]{1,0:T(8,128)S(1)}, f32[64,256]{1,0:T(8,128)S(1)}) fusion(f32[64,768]{1,0:T(8,128)S(1)} %get-tuple-element.11, f32[]{:T(128)} %bitcast.53, f32[]{:T(128)} %bitcast.52, f32[]{:T(128)} %bitcast.50, f32[]{:T(128)} %bitcast.56, f32[]{:T(128)} %bitcast.55, f32[]{:T(128)} %bitcast.54, ...), kind=kLoop, calls=%fused_computation.41 | loop fusion | flops 245760 | bytes 393252 | tf_op jit(solution)/shard_map/add | solution.py:87
  157.2 5.7 %multiply_add_fusion.8 = (f32[64,256]{1,0:T(8,128)S(1)}, f32[64,256]{1,0:T(8,128)S(1)}, f32[64,256]{1,0:T(8,128)S(1)}) fusion(f32[64,768]{1,0:T(8,128)S(1)} %get-tuple-element.13, f32[]{:T(128)} %bitcast.38, f32[]{:T(128)} %bitcast.37, f32[]{:T(128)} %bitcast.35, f32[]{:T(128)} %bitcast.41, f32[]{:T(128)} %bitcast.40, f32[]{:T(128)} %bitcast.39, ...), kind=kLoop, calls=%fused_computation.44 | loop fusion | flops 245760 | bytes 393252 | tf_op jit(solution)/shard_map/add | solution.py:87
  162.9 5.7 %multiply_add_fusion.11 = (f32[64,256]{1,0:T(8,128)S(1)}, f32[64,256]{1,0:T(8,128)S(1)}, f32[64,256]{1,0:T(8,128)S(1)}) fusion(f32[64,768]{1,0:T(8,128)S(1)} %get-tuple-element.14, f32[]{:T(128)} %bitcast.18, f32[]{:T(128)} %bitcast.17, f32[]{:T(128)} %bitcast.5, f32[]{:T(128)} %bitcast.21, f32[]{:T(128)} %bitcast.20, f32[]{:T(128)} %bitcast.19, ...), kind=kLoop, calls=%fused_computation.47 | loop fusion | flops 245760 | bytes 393252 | tf_op jit(solution)/shard_map/add | solution.py:87
  168.6 0.5 fusion.1
  169.2 5.7 %multiply_add_fusion.2 = (f32[64,256]{1,0:T(8,128)S(1)}, f32[64,256]{1,0:T(8,128)S(1)}, f32[64,256]{1,0:T(8,128)S(1)}) fusion(f32[64,768]{1,0:T(8,128)S(1)} %get-tuple-element.12, f32[]{:T(128)} %bitcast.68, f32[]{:T(128)} %bitcast.67, f32[]{:T(128)} %bitcast.65, f32[]{:T(128)} %bitcast.71, f32[]{:T(128)} %bitcast.70, f32[]{:T(128)} %bitcast.69, ...), kind=kLoop, calls=%fused_computation.38 | loop fusion | flops 245760 | bytes 393252 | tf_op jit(solution)/shard_map/add | solution.py:87
  174.9 1.6 fusion.17
  176.6 1.6 convolution_add_fusion.1
  178.2 1.1 fusion
  (17 shorter events, 0.2 us)
Async XLA Ops:
  6.5 139.5 %all-gather.3.cloned.1.call-start = ((), (), s32[]{:S(2)}) async-start(), calls=%async_computation | async-start | bytes 13369344 | tf_op jit(solution)/shard_map/all_gather | solution.py:67
  17.4 159.1 %collective-permute-start = (f32[768,256]{1,0:T(8,128)S(1)}, f32[768,256]{1,0:T(8,128)}, u32[]{:S(2)}, u32[]{:S(2)}) collective-permute-start(f32[768,256]{1,0:T(8,128)S(1)} %pad_maximum_fusion.1), channel_id=1, source_target_pairs={{0,15},{1,0},{2,1},{3,2},{4,3},{5,4},{6,5},{7,6},{8,7},{9,8},{10,9... | collective-permute-start | bytes 2359304 | tf_op jit(solution)/shard_map/ppermute | solution.py:13
  18.3 156.6 %collective-permute-start.2 = (f32[768,256]{1,0:T(8,128)S(1)}, f32[768,256]{1,0:T(8,128)}, u32[]{:S(2)}, u32[]{:S(2)}) collective-permute-start(f32[768,256]{1,0:T(8,128)S(1)} %pad_maximum_fusion.1), channel_id=1, source_target_pairs={{0,13},{1,14},{2,15},{3,0},{4,1},{5,2},{6,3},{7,4},{8,5},{9,6},{10... | collective-permute-start | bytes 2359304 | tf_op jit(solution)/shard_map/ppermute | solution.py:13
  19.2 159.0 %collective-permute-start.1 = (f32[768,256]{1,0:T(8,128)S(1)}, f32[768,256]{1,0:T(8,128)S(1)}, u32[]{:S(2)}, u32[]{:S(2)}) collective-permute-start(f32[768,256]{1,0:T(8,128)S(1)} %pad_maximum_fusion.1), channel_id=1, source_target_pairs={{0,14},{1,15},{2,0},{3,1},{4,2},{5,3},{6,4},{7,5},{8,6},{9,7},{10,... | collective-permute-start | bytes 2359304 | tf_op jit(solution)/shard_map/ppermute | solution.py:13
Sparse Core Ops, SparseCore 0:
  13.7 132.2 all-gather.2
